TPU v7x, 32 devices: a whole 2x2x4 slice. The times are simulated.
32 devices in a mesh: grp: 2 (over y), row: 4 (over z), head: 2 (over x), rep: 2 (over core).
Axes of the slice: x: 2, y: 2, z: 4, core: 2. Of those that a mesh axis runs over, the one named last changes fastest.
Arguments:
- queries: float32 [2048, 8192], P(('grp', 'row', 'rep'), 'head'), parts along dimension 0
- key_max: float32 [4096, 1024], P(('grp', 'row', 'rep'), 'head'), parts along dimension 0
- key_min: float32 [4096, 1024], P(('grp', 'row', 'rep'), 'head'), parts along dimension 0, as said below
- limits: int32 [2048], P(('grp', 'row', 'rep')), parts along dimension 0, may hold values from 0 to 2047, as said below
Outputs:
- page_mass: float32 [2048, 2048], P(('grp', 'row', 'rep'), 'head'), parts along dimension 0
There are 2 independent parts, one for each index of `grp`. A program takes and returns all parts, laid end to end along the dimension named above; each array names one. Nothing has to cross between parts.
Inputs may be any that keep to these rules, and one draw needn't show every extreme that they name: key_min <= key_max in every entry. Rows of the i-th aligned block of 128 rows have limits within the i-th block of 256 pages, not falling within a block; the first block's first row has the first page and the last block's last row the last page.
All inputs are finite; a program needn't handle non-finite values.
Results may differ from a plain program's by a relative error of at most 0.00013.
Values sent between devices are 32-bit elements; how exact they have to be, the bound alone decides.
No kernel may reach another device: no remote copies, remote signals or barrier semaphores. Data moves between devices by JAX's collectives and lax.ppermute only.
A program may use at most 64 MiB of HBM per device.

v0:
```python
import math
import jax
import jax.numpy as jnp
from jax import lax
from jax.sharding import PartitionSpec as P

DH = 128


def per_device(queries, key_max, key_min, limits):
    head_count = queries.shape[1] // DH
    kv_count = key_max.shape[1] // DH
    group_size = head_count // kv_count
    score_scale = 1.0 / math.sqrt(DH)
    bounds = jnp.stack((key_max, key_min))
    query_rows, row_limits = (queries, limits)
    gathered = lax.all_gather(bounds, ("row", "rep"), axis=1, tiled=True)
    page_ids = jnp.arange(gathered.shape[1], dtype=jnp.int32)
    row_count = query_rows.shape[0]
    page_count = gathered.shape[1]
    head_rows = query_rows.reshape(row_count, head_count, DH).transpose(1, 0, 2)
    positive = jnp.maximum(head_rows, 0.0)
    negative = jnp.minimum(head_rows, 0.0)
    sheets = gathered.reshape(2, page_count, kv_count, DH).transpose(2, 0, 1, 3)
    visible = page_ids[None, :] <= row_limits[:, None]

    def head_scores(head_index, kv_index):
        upper_part = jnp.dot(
            positive[head_index], sheets[kv_index, 0].T, precision=lax.Precision.HIGHEST
        )
        return upper_part + jnp.dot(
            negative[head_index], sheets[kv_index, 1].T, precision=lax.Precision.HIGHEST
        )

    def head_step(accumulated, head_index):
        raw_scores = head_scores(head_index, head_index // group_size)
        masked = jnp.where(visible, raw_scores * score_scale, -1e30)
        row_top = jnp.max(masked, axis=1, keepdims=True)
        weights = jnp.exp(masked - row_top)
        row_total = jnp.sum(weights, axis=1, keepdims=True)
        return (accumulated + weights / row_total, None)

    start = jnp.zeros((row_count, page_count), jnp.float32)
    accumulated, unused = lax.scan(head_step, start, jnp.arange(head_count, dtype=jnp.int32))
    return lax.psum_scatter(accumulated, "head", scatter_dimension=1, tiled=True)


def solution(mesh):
    placed = (
        P(("grp", "row", "rep"), "head"),
        P(("grp", "row", "rep"), "head"),
        P(("grp", "row", "rep"), "head"),
        P(("grp", "row", "rep")),
    )
    return jax.shard_map(
        per_device,
        mesh=mesh,
        in_specs=placed,
        out_specs=P(("grp", "row", "rep"), "head"),
        check_vma=False,
    )
```

profile of v0, /device:TPU:0, one launch (start us, length us, event | category | flops | bytes accessed | tf_op | source)
XLA Modules:
  0.0 448.6 jit_solution(9973003947528456110)
XLA Ops:
  14.3 80.7 %all-gather.2.cloned.1.call-done = f32[2,2048,512]{1,2,0:T(8,128)} async-done(((f32[2,256,512]{1,2,0:T(8,128)}), f32[2,2048,512]{1,2,0:T(8,128)}) %all-gather.2.cloned.1.call-update) | async-done | bytes 8388624 | tf_op jit(solution)/shard_map/all_gather | solution.py:17
  95.0 8.7 %copy.10 = f32[4,2,2048,128]{3,2,1,0:T(8,128)} copy(f32[4,2,2048,128]{2,3,0,1:T(8,128)} %bitcast.40) | data formatting | bytes 16777216
  103.8 318.0 %while.13 = (s32[]{:T(128)}, f32[128,2048]{1,0:T(8,128)S(1)}, s32[32]{0:T(128)S(1)}, f32[32,128,128]{1,2,0:T(8,128)}, f32[4,2,2048,128]{3,2,1,0:T(8,128)}, /*ind...) while((s32[]{:T(128)}, f32[128,2048]{1,0:T(8,128)S(1)}, ...), condition=%wide.region_3.4_spmd.clone, body=%wide.region_0.3_spmd.clone.sunk | while | flops 808189696 | bytes 9571716 | solution.py:44
  110.4 2.6 fusion.26
  120.4 2.6 fusion.26
  140.3 2.6 fusion.26
  160.1 2.6 fusion.26
  170.1 2.6 fusion.26
  180.0 2.6 fusion.26
  189.9 2.6 fusion.26
  199.9 2.6 fusion.26
  209.8 2.6 fusion.26
  219.7 2.6 fusion.26
  239.6 2.6 fusion.26
  259.5 2.6 fusion.26
  279.4 2.6 fusion.26
  299.2 2.6 fusion.26
  319.1 2.6 fusion.26
  339.0 2.6 fusion.26
  358.9 2.6 fusion.26
  378.7 2.6 fusion.26
  398.6 2.6 fusion.26
  418.5 2.6 fusion.26
  422.7 19.0 %reduce-scatter.2.cloned.1.call-done = f32[128,1024]{1,0:T(8,128)} async-done(((f32[128,2048]{1,0:T(8,128)}), f32[128,1024]{1,0:T(8,128)}) %reduce-scatter.2.cloned.1.call-update) | async-done | bytes 524304 | tf_op jit(solution)/shard_map/reduce_scatter | solution.py:45
  (155 shorter events, 154.2 us)
Async XLA Ops:
  6.5 88.5 %all-gather.2.cloned.1.call-start = ((), (), s32[]{:S(2)}) async-start(), calls=%async_computation.1 | async-start | bytes 9437184 | tf_op jit(solution)/shard_map/all_gather | solution.py:17
  10.1 431.6 %reduce-scatter.2.cloned.1.call-start = ((), (), s32[]{:S(2)}) async-start(), calls=%async_computation.2 | async-start | bytes 1572864 | tf_op jit(solution)/shard_map/reduce_scatter | solution.py:45
  95.0 8.8 %copy-start.1 = (s32[128]{0:T(128)S(1)}, s32[128]{0:T(128)}, u32[]{:S(2)}) copy-start(s32[128]{0:T(128)} %param.9) | copy-start | bytes 1540
  421.7 1.0 copy-start
Sparse Core Ops, SparseCore 0:
  10.2 84.7 all-gather.1
  422.9 18.8 reduce-scatter.1
where the time goes:
time: 452 us; the launch traced here: 449 us
  matrix products  157 us (35%)
  loops' own time  121 us (27%)
  waiting for transfers between devices  99.8 us (22%)
  local copies, waits for them, and re-layouts  33.2 us (7%)
  other arithmetic  24.4 us (5%)
  between operations  13.4 us (3%)
    another operation x1, loops' own time, per_device(): lax.scan(head_step, start, jnp.arange(head_count, dtype=jnp.int32))  121 us
    dot_general x32, matrix products, head_scores(): jnp.dot(negative[head_index], sheets[kv_index, 1].T, precision=lax.Precis...  82.2 us
    all_gather x1, waiting for transfers between devices, per_device(): gathered = lax.all_gather(bounds, ('row', 'rep'), axis=1, tiled=True)  80.7 us
    dot_general x32, matrix products, head_scores(): jnp.dot(positive[head_index], sheets[kv_index, 0].T, precision=lax.Precis...  74.5 us
    dynamic_slice x32, local copies, waits for them, and re-layouts, per_device(): lax.scan(head_step, start, jnp.arange(head_count, dtype=jnp.int32))  19.1 us
    reduce_scatter x1, waiting for transfers between devices, per_device(): lax.psum_scatter(accumulated, 'head', scatter_dimension=1, tiled=True)  19 us
    unnamed x8, local copies, waits for them, and re-layouts  14.1 us
    add x32, other arithmetic, head_step(): return (accumulated + weights / row_total, None)  11.5 us
  transfers between devices with their start and end apart: 2, of which 2 were waited for; matrix products, arithmetic and copies ran while one was open for 1% of the time, Pallas kernels for 0%

commit v1 on v0

--- a/solution.py
+++ b/solution.py
@@ -7,6 +7,24 @@
 DH = 128
 
 
+def tell_cells(x_local, mesh_ax):
+    extent = lax.axis_size(mesh_ax)
+    runs = []
+    for it in tuple(range(extent)):
+        runs.append((it, (it + 1) % extent))
+    leaves = []
+    for it in tuple(range(extent)):
+        leaves.append((it, (it - 1) % extent))
+    piece_out, back = ([x_local], [x_local])
+    for _ in range(extent // 2):
+        piece_out.append(lax.ppermute(piece_out[-1], perm=runs, axis_name=mesh_ax))
+    for _ in tuple(range((extent - 1) // 2)):
+        lower = lax.ppermute(back[-1], axis_name=mesh_ax, perm=leaves)
+        back.append(lower)
+    v_now = jnp.concatenate([*piece_out[::-1], *back[1:]], axis=1)
+    return jnp.roll(v_now, (lax.axis_index(mesh_ax) - extent // 2) * x_local.shape[1], axis=1)
+
+
 def per_device(queries, key_max, key_min, limits):
     head_count = queries.shape[1] // DH
     kv_count = key_max.shape[1] // DH
@@ -14,7 +32,7 @@
     score_scale = 1.0 / math.sqrt(DH)
     bounds = jnp.stack((key_max, key_min))
     query_rows, row_limits = (queries, limits)
-    gathered = lax.all_gather(bounds, ("row", "rep"), axis=1, tiled=True)
+    gathered = tell_cells(bounds, mesh_ax=("row", "rep"))
     page_ids = jnp.arange(gathered.shape[1], dtype=jnp.int32)
     row_count = query_rows.shape[0]
     page_count = gathered.shape[1]

time: 452 us -> 490 us (1.084)
  local copies, waits for them, and re-layouts: 33.2 us -> 54.5 us
  starting transfers between devices: 0.04 us -> 12.1 us
  loops' own time: 121 us -> 126 us
    all_gather x1 -> x0, waiting for transfers between devices: 80.7 us -> none  [per_device(): gathered = lax.all_gather(bounds, ('row', 'rep'), axis=1, tiled=True)]
    ppermute x0 -> x7, waiting for transfers between devices: none -> 71.7 us  [the longest x4 71.2 us: tell_cells(): piece_out.append(lax.ppermute(piece_out[-1], perm=runs, axis_name=mesh_ax))]
    unnamed x8 -> x33, local copies, waits for them, and re-layouts: 14.1 us -> 30.6 us
    ppermute x0 -> x7, starting transfers between devices: none -> 12.1 us  [the longest x3 11.6 us: tell_cells(): lower = lax.ppermute(back[-1], axis_name=mesh_ax, perm=leaves)]
    reduce_scatter x1, waiting for transfers between devices: 19 us -> 27 us  [per_device(): lax.psum_scatter(accumulated, 'head', scatter_dimension=1, tiled=True)]
  transfers between devices with their start and end apart: 2 -> 8, of which waited for: 2 -> 6; matrix products, arithmetic and copies ran while one was open for 1% -> 3% of each run, Pallas kernels for 0% -> 0%
where the time goes in v1:
time: 490 us; the launch traced here: 486 us
  matrix products  156 us (32%)
  loops' own time  126 us (26%)
  waiting for transfers between devices  98.7 us (20%)
  local copies, waits for them, and re-layouts  54.5 us (11%)
  other arithmetic  24.4 us (5%)
  between operations  13.7 us (3%)
  starting transfers between devices  12.1 us (2%)
    another operation x1, loops' own time, per_device(): lax.scan(head_step, start, jnp.arange(head_count, dtype=jnp.int32))  126 us
    dot_general x32, matrix products, head_scores(): jnp.dot(negative[head_index], sheets[kv_index, 1].T, precision=lax.Precis...  81.8 us
    dot_general x32, matrix products, head_scores(): jnp.dot(positive[head_index], sheets[kv_index, 0].T, precision=lax.Precis...  74.4 us
    ppermute x4, waiting for transfers between devices, tell_cells(): piece_out.append(lax.ppermute(piece_out[-1], perm=runs, axis_name=mesh_ax))  71.2 us
    unnamed x33, local copies, waits for them, and re-layouts  30.6 us
    reduce_scatter x1, waiting for transfers between devices, per_device(): lax.psum_scatter(accumulated, 'head', scatter_dimension=1, tiled=True)  27 us
    dynamic_slice x32, local copies, waits for them, and re-layouts, per_device(): lax.scan(head_step, start, jnp.arange(head_count, dtype=jnp.int32))  18.8 us
    ppermute x3, starting transfers between devices, tell_cells(): lower = lax.ppermute(back[-1], axis_name=mesh_ax, perm=leaves)  11.6 us
  transfers between devices with their start and end apart: 8, of which 6 were waited for; matrix products, arithmetic and copies ran while one was open for 3% of the time, Pallas kernels for 0%

profile of v1, /device:TPU:0, one launch (start us, length us, event | category | flops | bytes accessed | tf_op | source)
XLA Modules:
  0.0 485.6 jit_solution(18415792158599512535)
XLA Ops:
  9.8 4.1 collective-permute-start.4
  13.9 21.0 %collective-permute-done = f32[2,256,512]{1,2,0:T(8,128)S(1)} collective-permute-done((f32[2,256,512]{1,2,0:T(8,128)S(1)}, f32[2,256,512]{1,2,0:T(8,128)S(1)}, u32[]{:S(2)}, u32[]{:S(2)}) %collective-permute-start) | collective-permute-done | bytes 1048608 | tf_op jit(solution)/shard_map/ppermute | solution.py:20
  35.4 3.9 collective-permute-start.5
  39.3 19.2 %collective-permute-done.1 = f32[2,256,512]{1,2,0:T(8,128)} collective-permute-done((f32[2,256,512]{1,2,0:T(8,128)S(1)}, f32[2,256,512]{1,2,0:T(8,128)}, u32[]{:S(2)}, u32[]{:S(2)}) %collective-permute-start.1) | collective-permute-done | bytes 1048608 | tf_op jit(solution)/shard_map/ppermute | solution.py:20
  60.5 3.6 collective-permute-start.6
  64.1 14.6 %collective-permute-done.2 = f32[2,256,512]{1,2,0:T(8,128)} collective-permute-done((f32[2,256,512]{1,2,0:T(8,128)}, f32[2,256,512]{1,2,0:T(8,128)}, u32[]{:S(2)}, u32[]{:S(2)}) %collective-permute-start.2) | collective-permute-done | bytes 1048608 | tf_op jit(solution)/shard_map/ppermute | solution.py:20
  80.9 16.5 %collective-permute-done.3 = f32[2,256,512]{1,2,0:T(8,128)} collective-permute-done((f32[2,256,512]{1,2,0:T(8,128)}, f32[2,256,512]{1,2,0:T(8,128)}, u32[]{:S(2)}, u32[]{:S(2)}) %collective-permute-start.3) | collective-permute-done | bytes 1048608 | tf_op jit(solution)/shard_map/ppermute | solution.py:20
  116.7 3.8 constant_dynamic-slice_fusion
  120.5 8.7 %copy.10 = f32[4,2,2048,128]{3,2,1,0:T(8,128)} copy(f32[4,2,2048,128]{2,3,0,1:T(8,128)} %bitcast.40) | data formatting | bytes 16777216
  129.2 321.5 %while.13 = (s32[]{:T(128)}, f32[128,2048]{1,0:T(8,128)S(1)}, s32[32]{0:T(128)S(1)}, f32[32,128,128]{1,2,0:T(8,128)}, f32[4,2,2048,128]{3,2,1,0:T(8,128)}, /*ind...) while((s32[]{:T(128)}, f32[128,2048]{1,0:T(8,128)S(1)}, ...), condition=%wide.region_3.4_spmd.clone, body=%wide.region_0.3_spmd.clone.sunk | while | flops 808189696 | bytes 9571708 | solution.py:62
  136.0 2.6 fusion.26
  156.1 2.6 fusion.26
  176.2 2.6 fusion.26
  196.3 2.6 fusion.26
  216.4 2.6 fusion.26
  236.5 2.6 fusion.26
  256.6 2.6 fusion.26
  276.7 2.6 fusion.26
  296.8 2.6 fusion.26
  337.0 2.6 fusion.26
  377.2 2.6 fusion.26
  417.4 2.6 fusion.26
  447.5 2.6 fusion.26
  451.8 27.0 %reduce-scatter.2.cloned.1.call-done = f32[128,1024]{1,0:T(8,128)} async-done(((f32[128,2048]{1,0:T(8,128)}), f32[128,1024]{1,0:T(8,128)}) %reduce-scatter.2.cloned.1.call-update) | async-done | bytes 524304 | tf_op jit(solution)/shard_map/reduce_scatter | solution.py:63
  (195 shorter events, 190.4 us)
Async XLA Ops:
  6.5 472.2 %reduce-scatter.2.cloned.1.call-start = ((), (), s32[]{:S(2)}) async-start(), calls=%async_computation.1 | async-start | bytes 1572864 | tf_op jit(solution)/shard_map/reduce_scatter | solution.py:63
  7.8 73.1 %copy-start.1 = (f32[256,512]{0,1:T(8,128)}, f32[256,512]{0,1:T(8,128)S(1)}, u32[]{:S(2)}) copy-start(f32[256,512]{0,1:T(8,128)S(1)} %copy.6) | copy-start | bytes 1572868
  9.2 71.7 %copy-start.3 = (f32[256,512]{0,1:T(8,128)}, f32[256,512]{0,1:T(8,128)S(1)}, u32[]{:S(2)}) copy-start(f32[256,512]{0,1:T(8,128)S(1)} %copy.7) | copy-start | bytes 1572868
  9.3 25.6 %collective-permute-start = (f32[2,256,512]{1,2,0:T(8,128)S(1)}, f32[2,256,512]{1,2,0:T(8,128)S(1)}, u32[]{:S(2)}, u32[]{:S(2)}) collective-permute-start(f32[2,256,512]{1,2,0:T(8,128)S(1)} %pad_maximum_fusion), channel_id=1, source_target_pairs={{0,1},{1,4},{4,5},{5,8},{8,9},{9,12},{12,13},{13,0},{2,3},{3,6},{6... | collective-permute-start | bytes 3145736 | tf_op jit(solution)/shard_map/ppermute | solution.py:20
  9.8 25.6 %collective-permute-start.4 = (f32[2,256,512]{1,2,0:T(8,128)S(1)}, f32[2,256,512]{1,2,0:T(8,128)}, u32[]{:S(2)}, u32[]{:S(2)}) collective-permute-start(f32[2,256,512]{1,2,0:T(8,128)S(1)} %pad_maximum_fusion), channel_id=1, source_target_pairs={{0,13},{1,0},{4,1},{5,4},{8,5},{9,8},{12,9},{13,12},{2,15},{3,2},{... | collective-permute-start | bytes 3145736 | tf_op jit(solution)/shard_map/ppermute | solution.py:22
  34.9 23.6 %copy-start.5 = (f32[2,256,512]{1,2,0:T(8,128)}, f32[2,256,512]{1,2,0:T(8,128)S(1)}, u32[]{:S(2)}) copy-start(f32[2,256,512]{1,2,0:T(8,128)S(1)} %collective-permute-done) | copy-start | bytes 3145732
  34.9 23.6 %collective-permute-start.1 = (f32[2,256,512]{1,2,0:T(8,128)S(1)}, f32[2,256,512]{1,2,0:T(8,128)}, u32[]{:S(2)}, u32[]{:S(2)}) collective-permute-start(f32[2,256,512]{1,2,0:T(8,128)S(1)} %collective-permute-done), channel_id=1, source_target_pairs={{0,1},{1,4},{4,5},{5,8},{8,9},{9,12},{12,13},{13,0},{2,3},{3,6},{6... | collective-permute-start | bytes 3145736 | tf_op jit(solution)/shard_map/ppermute | solution.py:20
  35.4 25.0 %collective-permute-start.5 = (f32[2,256,512]{1,2,0:T(8,128)}, f32[2,256,512]{1,2,0:T(8,128)}, u32[]{:S(2)}, u32[]{:S(2)}) collective-permute-start(f32[2,256,512]{1,2,0:T(8,128)} %collective-permute-done.4), channel_id=1, source_target_pairs={{0,13},{1,0},{4,1},{5,4},{8,5},{9,8},{12,9},{13,12},{2,15},{3,2},{... | collective-permute-start | bytes 3145736 | tf_op jit(solution)/shard_map/ppermute | solution.py:22
  58.5 20.1 %collective-permute-start.2 = (f32[2,256,512]{1,2,0:T(8,128)}, f32[2,256,512]{1,2,0:T(8,128)}, u32[]{:S(2)}, u32[]{:S(2)}) collective-permute-start(f32[2,256,512]{1,2,0:T(8,128)} %collective-permute-done.1), channel_id=1, source_target_pairs={{0,1},{1,4},{4,5},{5,8},{8,9},{9,12},{12,13},{13,0},{2,3},{3,6},{6... | collective-permute-start | bytes 3145736 | tf_op jit(solution)/shard_map/ppermute | solution.py:20
  60.5 46.4 %collective-permute-start.6 = (f32[2,256,512]{1,2,0:T(8,128)}, f32[2,256,512]{1,2,0:T(8,128)}, u32[]{:S(2)}, u32[]{:S(2)}) collective-permute-start(f32[2,256,512]{1,2,0:T(8,128)} %collective-permute-done.5), channel_id=1, source_target_pairs={{0,13},{1,0},{4,1},{5,4},{8,5},{9,8},{12,9},{13,12},{2,15},{3,2},{... | collective-permute-start | bytes 3145736 | tf_op jit(solution)/shard_map/ppermute | solution.py:22
  78.7 18.7 %collective-permute-start.3 = (f32[2,256,512]{1,2,0:T(8,128)}, f32[2,256,512]{1,2,0:T(8,128)}, u32[]{:S(2)}, u32[]{:S(2)}) collective-permute-start(f32[2,256,512]{1,2,0:T(8,128)} %collective-permute-done.2), channel_id=1, source_target_pairs={{0,1},{1,4},{4,5},{5,8},{8,9},{9,12},{12,13},{13,0},{2,3},{3,6},{6... | collective-permute-start | bytes 3145736 | tf_op jit(solution)/shard_map/ppermute | solution.py:20
  80.9 31.4 %copy-start.6 = (f32[2,256,512]{1,2,0:T(8,128)S(1)}, f32[2,256,512]{1,2,0:T(8,128)}, u32[]{:S(2)}) copy-start(f32[2,256,512]{1,2,0:T(8,128)} %copy-done.5) | copy-start | bytes 3145732
  80.9 31.6 %copy-start.2 = (f32[256,512]{0,1:T(8,128)S(1)}, f32[256,512]{0,1:T(8,128)}, u32[]{:S(2)}) copy-start(f32[256,512]{0,1:T(8,128)} %copy-done.1) | copy-start | bytes 1572868
  80.9 31.6 %copy-start.4 = (f32[256,512]{0,1:T(8,128)S(1)}, f32[256,512]{0,1:T(8,128)}, u32[]{:S(2)}) copy-start(f32[256,512]{0,1:T(8,128)} %copy-done.3) | copy-start | bytes 1572868
  116.7 12.6 %copy-start.7 = (s32[128]{0:T(128)S(1)}, s32[128]{0:T(128)}, u32[]{:S(2)}) copy-start(s32[128]{0:T(128)} %param.9) | copy-start | bytes 1540
  450.8 1.0 copy-start
Sparse Core Ops, SparseCore 0:
  451.9 26.8 reduce-scatter.1
